TPU v7x, 128 devices: a whole 4x4x4 slice. The times are simulated.
128 devices in a mesh: dp: 4 (over y_hi, core), head: 4 (over x), ctx: 8 (over z, y_lo).
Axes of the slice: x: 4, y: 4 (y_hi: 2, y_lo: 2; y = y_hi * 2 + y_lo), z: 4, core: 2. Of those that a mesh axis runs over, the one named last changes fastest.
Arguments:
- video: bfloat16 [16, 64, 24576], P('dp', 'head', 'ctx'), parts along dimension 0, may hold values from -6 to 6
- cache: bfloat16 [8, 64, 24576], P('dp', 'head', 'ctx'), parts along dimension 0, may hold values from -6 to 6
- conv_weight: bfloat16 [3, 3, 288, 192], replicated, may hold values from -0.125 to 0.125
- conv_bias: float32 [192], replicated, may hold values from -3 to 3
- down_weight: bfloat16 [768, 192], replicated, may hold values from -0.21875 to 0.21875
- patch_weight: bfloat16 [768, 5120], P(None, ('head', 'ctx')), may hold values from -0.21875 to 0.21875
- step_index: int32 [4], P('dp'), parts along dimension 0, may hold values from 0 to 999
- mod_weight: bfloat16 [256, 10240], P(None, ('head', 'ctx')), may hold values from -1 to 1
- qkv_weight: bfloat16 [5120, 20, 3, 128], P('ctx', 'head'), may hold values from -0.078125 to 0.078125
Outputs:
- attended: bfloat16 [16384, 2560], P(('dp', 'ctx'), 'head'), parts along dimension 0
There are 4 independent parts, one for each index of `dp`. A program takes and returns all parts, laid end to end along the dimension named above; an argument that names none is the same for every part. Nothing has to cross between parts.
All inputs are finite; a program needn't handle non-finite values.
Results may differ from a plain program's by a relative error of at most 0.015.
The roundings to bfloat16 on the way count: a program that leaves them out, or rounds other values in their place, can miss the bound.
Values may be sent and summed in bfloat16 or wider, within the bound.
No kernel may reach another device: no remote copies, remote signals or barrier semaphores. Data moves between devices by JAX's collectives and lax.ppermute only.
A program may use at most 128 MiB of HBM per device.

v0:
```python
import jax
import jax.numpy as jnp
from jax import lax
from jax.sharding import PartitionSpec as P

D = 5120
HDIM = 128
FREQ = 256


def with_halo(cells, sides, width):
    for axis, dim in sides:
        count = lax.axis_size(axis)
        ends = count - 1
        head = lax.slice_in_dim(cells, 0, width, axis=dim)
        tail = lax.slice_in_dim(cells, cells.shape[dim] - width, cells.shape[dim], axis=dim)
        cells = jnp.concatenate(
            [
                lax.ppermute(tail, axis, [(i, (i + 1) % count) for i in range(ends)]),
                cells,
                lax.ppermute(head, axis, [((i + 1) % count, i) for i in range(ends)]),
            ],
            axis=dim,
        )
    return cells


def silu_act(value):
    return value * jax.nn.sigmoid(value)


def shards(
    video,
    cache,
    conv_weight,
    conv_bias,
    down_weight,
    patch_weight,
    step_index,
    mod_weight,
    qkv_weight,
):
    cin = conv_weight.shape[2] // 3
    cmid = conv_weight.shape[3]
    frame_count = video.shape[0]
    tile_rows = video.shape[1]
    tile_cols = video.shape[2] // cin
    frames = jnp.concatenate([cache, video], 0).reshape(frame_count + 2, tile_rows, tile_cols, cin)
    padded = with_halo(frames, (("head", 1), ("ctx", 2)), 1)
    total = jnp.zeros((frame_count, tile_rows, tile_cols, cmid), jnp.float32)
    for time_tap in range(3):
        for row_tap in range(3):
            slab = padded[time_tap : time_tap + frame_count, row_tap : row_tap + tile_rows]
            stacked = jnp.concatenate(
                [slab[:, :, col_tap : col_tap + tile_cols] for col_tap in range(3)], -1
            )
            total = total + jnp.einsum(
                "fyxc,cd->fyxd",
                stacked,
                conv_weight[time_tap, row_tap],
                preferred_element_type=jnp.float32,
            )
    hidden = silu_act(total + conv_bias).astype(jnp.bfloat16)
    stacked = (
        hidden.reshape(frame_count, tile_rows // 2, 2, tile_cols // 2, 2, cmid)
        .transpose(0, 1, 3, 2, 4, 5)
        .reshape(-1, 4 * cmid)
    )
    reduced = silu_act(jnp.dot(stacked, down_weight, preferred_element_type=jnp.float32)).astype(
        jnp.bfloat16
    )
    reduced = reduced.reshape(frame_count, tile_rows // 2, tile_cols // 2, cmid)
    patches = reduced.reshape(frame_count, tile_rows // 4, 2, tile_cols // 4, 2, cmid).transpose(
        0, 1, 3, 2, 4, 5
    )
    patches = patches.reshape(-1, 4 * cmid)
    half = FREQ // 2
    freqs = jnp.exp(-jnp.log(10000.0) * jnp.arange(half, dtype=jnp.float32) / half)
    angles = step_index[0].astype(jnp.float32) * freqs
    timing = jnp.concatenate([jnp.cos(angles), jnp.sin(angles)]).astype(jnp.bfloat16)
    mod_share = jnp.dot(timing[None, :], mod_weight, preferred_element_type=jnp.float32)[0]
    modulation = lax.all_gather(mod_share, ("head", "ctx"), axis=0, tiled=True)
    scale = modulation[:D]
    shift = modulation[D:]
    embedded = jnp.dot(
        patches,
        lax.all_gather(patch_weight, ("head", "ctx"), axis=1, tiled=True),
        preferred_element_type=jnp.float32,
    )
    inverse = lax.rsqrt(jnp.mean(embedded * embedded, -1, keepdims=True) + 1e-06)
    normed = (embedded * inverse * (1.0 + scale) + shift).astype(jnp.bfloat16)
    gathered = lax.all_gather(normed, "head", axis=0, tiled=True)
    group_rows = gathered.shape[0]
    heads_here = qkv_weight.shape[1]
    out_cols = heads_here * 3 * HDIM
    piece = lax.all_gather(qkv_weight, "ctx", axis=0, tiled=True)
    qkv = jnp.dot(
        gathered, piece.reshape(piece.shape[0], out_cols), preferred_element_type=jnp.float32
    )
    qkv = qkv.astype(jnp.bfloat16).reshape(group_rows, heads_here, 3, HDIM)
    query = qkv[:, :, 0]
    keys = qkv[:, :, 1]
    values = qkv[:, :, 2]
    inv_root = 1.0 / jnp.sqrt(jnp.float32(HDIM))
    best = jnp.full((heads_here, group_rows), -1e30, jnp.float32)
    key_piece = lax.all_gather(keys, "ctx", axis=0, tiled=True)
    value_piece = lax.all_gather(values, "ctx", axis=0, tiled=True)
    scores = (
        jnp.einsum("qhd,khd->hqk", query, key_piece, preferred_element_type=jnp.float32) * inv_root
    )
    new_best = jnp.maximum(best, jnp.max(scores, -1))
    probs = jnp.exp(scores - new_best[..., None])
    denom = jnp.sum(probs, -1)
    accum = jnp.einsum(
        "hqk,khd->hqd", probs.astype(jnp.bfloat16), value_piece, preferred_element_type=jnp.float32
    )
    best, denom, accum = (new_best, denom, accum)
    result = (accum / denom[..., None]).astype(jnp.bfloat16)
    return result.transpose(1, 0, 2).reshape(group_rows, heads_here * HDIM)


def solution(mesh):
    return jax.shard_map(
        shards,
        mesh=mesh,
        in_specs=(
            P("dp", "head", "ctx"),
            P("dp", "head", "ctx"),
            P(),
            P(),
            P(),
            P(None, ("head", "ctx")),
            P("dp"),
            P(None, ("head", "ctx")),
            P("ctx", "head", None, None),
        ),
        out_specs=P(("dp", "ctx"), "head"),
        check_vma=False,
    )
```

profile of v0, /device:TPU:1, one launch (start us, length us, event | category | flops | bytes accessed | tf_op | source)
XLA Modules:
  0.0 923.7 jit_solution(17581543572212077937)
XLA Ops:
  10.8 4.6 collective-permute-start
  15.3 1.3 collective-permute-start.1
  19.2 141.1 %all-reduce = f32[10240]{0:T(1024)S(1)} all-reduce(f32[10240]{0:T(1024)S(1)} %dynamic-update-slice), channel_id=1, replica_groups=mesh['dp'=4,'head'=4,'ctx'=8] {'head','ctx'}, use_global_device_ids=true, to_apply=%add | all-reduce | flops 10240 | bytes 81920
  164.3 1.3 collective-permute-start.2
  165.6 1.5 collective-permute-start.3
  167.6 1.4 collective-permute-done.2
  168.9 1.9 fusion.81
  170.8 1.3 collective-permute-done.3
  172.1 2.1 fusion.73
  181.5 2.6 multiply_convert_fusion
  187.7 8.9 all-gather.8.cloned.1.call-done
  196.7 5.9 multiply_reduce_fusion.1
  202.6 1.5 add_convert_fusion
  204.8 3.1 copy.17
  208.0 63.2 %all-gather.10.cloned.1.call-done = bf16[512,5120]{1,0:T(8,128)(2,1)} async-done(((bf16[128,5120]{1,0:T(8,128)(2,1)}), bf16[512,5120]{1,0:T(8,128)(2,1)}) %all-gather.10.cloned.1.call-update) | async-done | bytes 5242896 | tf_op jit(solution)/shard_map/all_gather | solution.py:92
  271.2 381.9 %all-gather.12.cloned.1.call-done = bf16[5120,5,3,128]{0,3,2,1:T(8,128)(2,1)} async-done(((bf16[640,5,3,128]{0,3,2,1:T(8,128)(2,1)}), bf16[5120,5,3,128]{0,3,2,1:T(8,128)(2,1)}) %all-gather.12.cloned.1.call-update) | async-done | bytes 19660816 | tf_op jit(solution)/shard_map/all_gather | solution.py:96
  653.1 17.7 %convolution_convert_fusion = bf16[512,1920]{1,0:T(8,128)(2,1)} fusion(bf16[512,5120]{1,0:T(8,128)(2,1)} %all-gather.10.cloned.1.call-done, bf16[5120,1920]{0,1:T(8,128)(2,1)} %bitcast.113), kind=kOutput, calls=%fused_computation.24 | convolution fusion | flops 10067312640 | bytes 26869760 | tf_op jit(solution)/shard_map/dot_general | solution.py:97
  670.8 2.7 copy.18
  674.5 1.1 copy.33
  676.2 110.6 %all-gather.14.cloned.1.call-done = bf16[4096,5,1,128]{3,0,1,2:T(8,128)(2,1)} async-done(((bf16[512,5,1,128]{3,0,1,2:T(8,128)(2,1)}), bf16[4096,5,1,128]{3,0,1,2:T(8,128)(2,1)}) %all-gather.14.cloned.1.call-update) | async-done | bytes 5242896 | tf_op jit(solution)/shard_map/all_gather | solution.py:106
  786.8 19.0 %multiply_reduce_fusion = (f32[5,512]{1,0:T(8,128)S(1)}, f32[5,512,4096]{2,1,0:T(8,128)}) fusion(bf16[4096,5,1,128]{3,0,1,2:T(8,128)(2,1)} %all-gather.14.cloned.1.call-done, bf16[512,5,3,128]{0,3,2,1:T(8,128)(2,1)S(1)} %bitcast.108), kind=kOutput, calls=%fused_computation.1 | convolution fusion | flops 2705323520 | bytes 47851520 | tf_op jit(solution)/shard_map/qhd,khd->hqk/dot_general | solution.py:109
  805.8 17.3 %fusion = f32[5,512]{1,0:T(8,128)S(1)} fusion(f32[5,512,4096]{2,1,0:T(8,128)} %get-tuple-element.47, f32[5,512]{1,0:T(8,128)S(1)} %broadcast_maximum_fusion), kind=kLoop, calls=%fused_computation.2 | loop fusion | flops 31454720 | bytes 41963520 | tf_op jit(solution)/shard_map/reduce_sum | solution.py:113
  823.2 75.6 %all-gather.16.cloned.1.call-done = bf16[4096,5,1,128]{0,3,1,2:T(8,128)(2,1)} async-done(((bf16[512,5,1,128]{0,3,1,2:T(8,128)(2,1)}), bf16[4096,5,1,128]{0,3,1,2:T(8,128)(2,1)}) %all-gather.16.cloned.1.call-update) | async-done | bytes 5242896 | tf_op jit(solution)/shard_map/all_gather | solution.py:107
  898.7 17.3 %divide_convert_fusion = bf16[512,5,128]{0,2,1:T(8,128)(2,1)S(1)} fusion(bf16[4096,5,1,128]{0,3,1,2:T(8,128)(2,1)} %all-gather.16.cloned.1.call-done, f32[5,512,4096]{2,1,0:T(8,128)} %get-tuple-element.47, f32[5,512]{1,0:T(8,128)S(1)} %broadcast_maximum_fusion, f32[512,5]{0,1:T(8,128)S(1)} %bitcast.112), kind=kOutput, calls=%fused_computation.84 | convolution fusion | flops 2716467200 | bytes 47861760 | tf_op jit(solution)/shard_map/hqk,khd->hqd/dot_general | solution.py:114
  (70 shorter events, 23.9 us)
Async XLA Ops:
  6.5 180.0 %copy-start = (bf16[768,192]{0,1:T(8,128)(2,1)S(1)}, bf16[768,192]{0,1:T(8,128)(2,1)}, u32[]{:S(2)}) copy-start(bf16[768,192]{0,1:T(8,128)(2,1)} %param.13) | copy-start | bytes 884740
  6.5 10.8 %copy-start.7 = (u32[128]{0:T(128)S(1)}, u32[128]{0:T(128)}, u32[]{:S(2)}) copy-start(u32[128]{0:T(128)} %constant.27) | copy-start | bytes 1540
  6.5 12.2 %copy-start.4 = (bf16[256,320]{0,1:T(8,128)(2,1)S(1)}, bf16[256,320]{0,1:T(8,128)(2,1)}, u32[]{:S(2)}) copy-start(bf16[256,320]{0,1:T(8,128)(2,1)} %param.16) | copy-start | bytes 491524
  6.5 190.1 %all-gather.8.cloned.1.call-start = ((), (), s32[]{:S(2)}) async-start(), calls=%async_computation | async-start | bytes 8110080 | tf_op jit(solution)/shard_map/all_gather | solution.py:87
  7.3 264.0 %all-gather.10.cloned.1.call-start = ((), (), s32[]{:S(2)}) async-start(), calls=%async_computation.1 | async-start | bytes 6553600 | tf_op jit(solution)/shard_map/all_gather | solution.py:92
  8.3 152.2 %copy-start.3 = (bf16[4,16,3072]{2,1,0:T(8,128)(2,1)S(1)}, bf16[4,16,3072]{2,1,0:T(8,128)(2,1)}, u32[]{:S(2)}) copy-start(bf16[4,16,3072]{2,1,0:T(8,128)(2,1)} %param.9) | copy-start | bytes 1179652
  10.8 151.3 %collective-permute-start = (bf16[6,1,32,96]{3,2,1,0:T(8,128)(2,1)}, bf16[6,1,32,96]{3,2,1,0:T(8,128)(2,1)}, u32[]{:S(2)}, u32[]{:S(2)}) collective-permute-start(bf16[6,1,32,96]{3,2,1,0:T(8,128)(2,1)} %get-tuple-element.35), channel_id=1, source_target_pairs={{0,8},{8,16},{16,24},{1,9},{9,17},{17,25},{2,10},{10,18},{18,26},{... | collective-permute-start | bytes 110600 | tf_op jit(solution)/shard_map/ppermute | solution.py:19
  15.3 148.0 %collective-permute-start.1 = (bf16[6,1,32,96]{3,2,1,0:T(8,128)(2,1)}, bf16[6,1,32,96]{3,2,1,0:T(8,128)(2,1)}, u32[]{:S(2)}, u32[]{:S(2)}) collective-permute-start(bf16[6,1,32,96]{3,2,1,0:T(8,128)(2,1)} %get-tuple-element.34), channel_id=1, source_target_pairs={{8,0},{16,8},{24,16},{9,1},{17,9},{25,17},{10,2},{18,10},{26,18},{... | collective-permute-start | bytes 110600 | tf_op jit(solution)/shard_map/ppermute | solution.py:21
  164.3 4.6 collective-permute-start.2
  165.6 6.5 collective-permute-start.3
  170.8 3.4 copy-start.5
  180.5 0.9 copy-start.6
  202.6 2.2 copy-start.2
  204.1 449.0 %all-gather.12.cloned.1.call-start = ((), (), s32[]{:S(2)}) async-start(), calls=%async_computation.2 | async-start | bytes 22118400 | tf_op jit(solution)/shard_map/all_gather | solution.py:96
  207.9 578.8 %all-gather.14.cloned.1.call-start = ((), (), s32[]{:S(2)}) async-start(), calls=%async_computation.3 | async-start | bytes 5898240 | tf_op jit(solution)/shard_map/all_gather | solution.py:106
  675.6 223.2 %all-gather.16.cloned.1.call-start = ((), (), s32[]{:S(2)}) async-start(), calls=%async_computation.4 | async-start | bytes 5898240 | tf_op jit(solution)/shard_map/all_gather | solution.py:107
  898.7 18.4 %copy-start.1 = (bf16[768,192]{0,1:T(8,128)(2,1)S(1)}, bf16[768,192]{0,1:T(8,128)(2,1)}, u32[]{:S(2)}) copy-start(bf16[768,192]{0,1:T(8,128)(2,1)} %param.13) | copy-start | bytes 884740
Sparse Core Ops, SparseCore 0:
  9.0 187.6 all-gather.7
  204.2 66.9 all-gather.9
  272.9 380.1 all-gather.11
  675.7 111.0 all-gather.13
  788.3 110.4 all-gather.15
where the time goes:
time: 924 us
  waiting for transfers between devices  644 us (70%)
  blocking collectives  141 us (15%)
  matrix products  70.4 us (8%)
  other arithmetic  22.9 us (2%)
  local copies, waits for them, and re-layouts  21.4 us (2%)
  between operations  14.9 us (2%)
    all_gather x1, waiting for transfers between devices, shards(): piece = lax.all_gather(qkv_weight, 'ctx', axis=0, tiled=True)  382 us
    unnamed x1, blocking collectives  141 us
    all_gather x1, waiting for transfers between devices, shards(): key_piece = lax.all_gather(keys, 'ctx', axis=0, tiled=True)  111 us
    all_gather x1, waiting for transfers between devices, shards(): value_piece = lax.all_gather(values, 'ctx', axis=0, tiled=True)  75.6 us
    all_gather x1, waiting for transfers between devices, shards(): gathered = lax.all_gather(normed, 'head', axis=0, tiled=True)  63.2 us
    dot_general x1, matrix products, shards(): jnp.einsum('qhd,khd->hqk', query, key_piece, preferred_element_type=jnp.f...  19 us
  transfers between devices with their start and end apart: 9, of which 7 were waited for; matrix products, arithmetic and copies ran while one was open for 7% of the time, Pallas kernels for 0%

commit v1 on v0

--- a/solution.py
+++ b/solution.py
@@ -103,8 +103,11 @@
     values = qkv[:, :, 2]
     inv_root = 1.0 / jnp.sqrt(jnp.float32(HDIM))
     best = jnp.full((heads_here, group_rows), -1e30, jnp.float32)
-    key_piece = lax.all_gather(keys, "ctx", axis=0, tiled=True)
-    value_piece = lax.all_gather(values, "ctx", axis=0, tiled=True)
+    key_piece, value_piece = jnp.split(
+        lax.all_gather(jnp.concatenate([keys, values], axis=1), "ctx", tiled=True, axis=0),
+        [keys.shape[1]],
+        axis=1,
+    )
     scores = (
         jnp.einsum("qhd,khd->hqk", query, key_piece, preferred_element_type=jnp.float32) * inv_root
     )

time: 924 us -> 953 us (1.031)
  waiting for transfers between devices: 644 us -> 670 us
    all_gather x2 -> x1, waiting for transfers between devices: 186 us -> 209 us  [shards(): lax.all_gather(jnp.concatenate([keys, values], axis=1), 'ctx', tiled=True...]
  transfers between devices with their start and end apart: 9 -> 8, of which waited for: 7 -> 5; matrix products, arithmetic and copies ran while one was open for 7% -> 3% of each run, Pallas kernels for 0% -> 0%
where the time goes in v1:
time: 953 us; the launch traced here: 952 us
  waiting for transfers between devices  670 us (70%)
  blocking collectives  138 us (14%)
  matrix products  70.9 us (7%)
  other arithmetic  25.2 us (3%)
  local copies, waits for them, and re-layouts  24.1 us (3%)
  between operations  14.8 us (2%)
    all_gather x1, waiting for transfers between devices, shards(): piece = lax.all_gather(qkv_weight, 'ctx', axis=0, tiled=True)  382 us
    all_gather x1, waiting for transfers between devices, shards(): lax.all_gather(jnp.concatenate([keys, values], axis=1), 'ctx', tiled=True...  209 us
    unnamed x1, blocking collectives  138 us
    all_gather x1, waiting for transfers between devices, shards(): gathered = lax.all_gather(normed, 'head', axis=0, tiled=True)  63.6 us
  transfers between devices with their start and end apart: 8, of which 5 were waited for; matrix products, arithmetic and copies ran while one was open for 3% of the time, Pallas kernels for 0%

profile of v1, /device:TPU:1, one launch (start us, length us, event | category | flops | bytes accessed | tf_op | source)
XLA Modules:
  0.0 951.8 jit_solution(2672845709657614051)
XLA Ops:
  10.8 1.3 collective-permute-start.1
  12.1 5.2 collective-permute-start
  19.7 137.9 %all-reduce = f32[10240]{0:T(1024)S(1)} all-reduce(f32[10240]{0:T(1024)S(1)} %dynamic-update-slice), channel_id=1, replica_groups=mesh['dp'=4,'head'=4,'ctx'=8] {'head','ctx'}, use_global_device_ids=true, to_apply=%add | all-reduce | flops 10240 | bytes 81920
  161.5 1.3 collective-permute-start.2
  162.8 1.5 collective-permute-start.3
  164.8 4.4 collective-permute-done.3
  169.3 2.2 fusion.73
  171.5 1.9 fusion.81
  180.6 2.6 multiply_convert_fusion
  186.9 10.2 %all-gather.5.cloned.1.call-done = bf16[768,5120]{0,1:T(8,128)(2,1)} async-done(((bf16[768,160]{0,1:T(8,128)(2,1)}), bf16[768,5120]{0,1:T(8,128)(2,1)}) %all-gather.5.cloned.1.call-update) | async-done | bytes 7864336 | tf_op jit(solution)/shard_map/all_gather | solution.py:87
  197.0 5.9 multiply_reduce_fusion.1
  203.0 1.5 add_convert_fusion
  205.2 3.1 copy.18
  208.4 63.6 %all-gather.7.cloned.1.call-done = bf16[512,5120]{1,0:T(8,128)(2,1)} async-done(((bf16[128,5120]{1,0:T(8,128)(2,1)}), bf16[512,5120]{1,0:T(8,128)(2,1)}) %all-gather.7.cloned.1.call-update) | async-done | bytes 5242896 | tf_op jit(solution)/shard_map/all_gather | solution.py:92
  271.9 381.9 %all-gather.9.cloned.1.call-done = bf16[5120,5,3,128]{0,3,2,1:T(8,128)(2,1)} async-done(((bf16[640,5,3,128]{0,3,2,1:T(8,128)(2,1)}), bf16[5120,5,3,128]{0,3,2,1:T(8,128)(2,1)}) %all-gather.9.cloned.1.call-update) | async-done | bytes 19660816 | tf_op jit(solution)/shard_map/all_gather | solution.py:96
  653.8 17.7 %convolution_convert_fusion = bf16[512,1920]{1,0:T(8,128)(2,1)} fusion(bf16[512,5120]{1,0:T(8,128)(2,1)} %all-gather.7.cloned.1.call-done, bf16[5120,1920]{0,1:T(8,128)(2,1)} %bitcast.103), kind=kOutput, calls=%fused_computation.24 | convolution fusion | flops 10067312640 | bytes 26869760 | tf_op jit(solution)/shard_map/dot_general | solution.py:97
  671.6 2.7 copy.19
  675.5 1.4 copy.36
  676.9 2.2 copy.37
  679.1 2.3 pad_maximum_fusion.2
  681.4 208.8 %all-gather.11.cloned.1.call-done = bf16[4096,10,128]{2,0,1:T(8,128)(2,1)} async-done(((bf16[512,10,128]{2,0,1:T(8,128)(2,1)}), bf16[4096,10,128]{2,0,1:T(8,128)(2,1)}) %all-gather.11.cloned.1.call-update) | async-done | bytes 10485776 | tf_op jit(solution)/shard_map/all_gather | solution.py:107
  890.2 18.8 %multiply_reduce_fusion = (f32[5,512]{1,0:T(8,128)S(1)}, f32[5,512,4096]{2,1,0:T(8,128)}) fusion(bf16[4096,10,128]{2,0,1:T(8,128)(2,1)} %all-gather.11.cloned.1.call-done, bf16[512,5,3,128]{0,3,2,1:T(8,128)(2,1)S(1)} %bitcast.96), kind=kOutput, calls=%fused_computation.1 | convolution fusion | flops 2705323520 | bytes 47851520 | tf_op jit(solution)/shard_map/qhd,khd->hqk/dot_general | solution.py:112
  909.0 17.2 %fusion = f32[5,512]{1,0:T(8,128)S(1)} fusion(f32[5,512,4096]{2,1,0:T(8,128)} %get-tuple-element.47, f32[5,512]{1,0:T(8,128)S(1)} %broadcast_maximum_fusion), kind=kLoop, calls=%fused_computation.2 | loop fusion | flops 31454720 | bytes 41963520 | tf_op jit(solution)/shard_map/reduce_sum | solution.py:116
  926.2 18.0 %divide_convert_fusion = bf16[512,5,128]{0,2,1:T(8,128)(2,1)S(1)} fusion(bf16[4096,10,128]{2,0,1:T(8,128)(2,1)} %all-gather.11.cloned.1.call-done, f32[5,512,4096]{2,1,0:T(8,128)} %get-tuple-element.47, f32[5,512]{1,0:T(8,128)S(1)} %broadcast_maximum_fusion, f32[512,5]{0,1:T(8,128)S(1)} %bitcast.102), kind=kOutput, calls=%fused_computation.85 | convolution fusion | flops 2716467200 | bytes 47861760 | tf_op jit(solution)/shard_map/hqk,khd->hqd/dot_general | solution.py:117
  (69 shorter events, 23.5 us)
Async XLA Ops:
  6.5 179.2 %copy-start = (bf16[768,192]{0,1:T(8,128)(2,1)S(1)}, bf16[768,192]{0,1:T(8,128)(2,1)}, u32[]{:S(2)}) copy-start(bf16[768,192]{0,1:T(8,128)(2,1)} %param.13) | copy-start | bytes 884740
  6.5 11.5 %copy-start.7 = (u32[128]{0:T(128)S(1)}, u32[128]{0:T(128)}, u32[]{:S(2)}) copy-start(u32[128]{0:T(128)} %constant.27) | copy-start | bytes 1540
  6.5 12.6 %copy-start.4 = (bf16[256,320]{0,1:T(8,128)(2,1)S(1)}, bf16[256,320]{0,1:T(8,128)(2,1)}, u32[]{:S(2)}) copy-start(bf16[256,320]{0,1:T(8,128)(2,1)} %param.16) | copy-start | bytes 491524
  6.5 190.5 %all-gather.5.cloned.1.call-start = ((), (), s32[]{:S(2)}) async-start(), calls=%async_computation | async-start | bytes 8110080 | tf_op jit(solution)/shard_map/all_gather | solution.py:87
  7.3 264.7 %all-gather.7.cloned.1.call-start = ((), (), s32[]{:S(2)}) async-start(), calls=%async_computation.1 | async-start | bytes 6553600 | tf_op jit(solution)/shard_map/all_gather | solution.py:92
  8.3 149.4 %copy-start.3 = (bf16[4,16,3072]{2,1,0:T(8,128)(2,1)S(1)}, bf16[4,16,3072]{2,1,0:T(8,128)(2,1)}, u32[]{:S(2)}) copy-start(bf16[4,16,3072]{2,1,0:T(8,128)(2,1)} %param.9) | copy-start | bytes 1179652
  10.8 149.8 %collective-permute-start.1 = (bf16[6,1,32,96]{3,2,1,0:T(8,128)(2,1)}, bf16[6,1,32,96]{3,2,1,0:T(8,128)(2,1)}, u32[]{:S(2)}, u32[]{:S(2)}) collective-permute-start(bf16[6,1,32,96]{3,2,1,0:T(8,128)(2,1)} %get-tuple-element.34), channel_id=1, source_target_pairs={{8,0},{16,8},{24,16},{9,1},{17,9},{25,17},{10,2},{18,10},{26,18},{... | collective-permute-start | bytes 110600 | tf_op jit(solution)/shard_map/ppermute | solution.py:21
  12.1 147.2 %collective-permute-start = (bf16[6,1,32,96]{3,2,1,0:T(8,128)(2,1)}, bf16[6,1,32,96]{3,2,1,0:T(8,128)(2,1)}, u32[]{:S(2)}, u32[]{:S(2)}) collective-permute-start(bf16[6,1,32,96]{3,2,1,0:T(8,128)(2,1)} %get-tuple-element.35), channel_id=1, source_target_pairs={{0,8},{8,16},{16,24},{1,9},{9,17},{17,25},{2,10},{10,18},{18,26},{... | collective-permute-start | bytes 110600 | tf_op jit(solution)/shard_map/ppermute | solution.py:19
  161.5 10.0 %collective-permute-start.2 = (bf16[6,18,1,96]{3,2,1,0:T(2,128)(2,1)S(1)}, bf16[6,18,1,96]{3,2,1,0:T(2,128)(2,1)S(1)}, u32[]{:S(2)}, u32[]{:S(2)}) collective-permute-start(bf16[6,18,1,96]{3,2,1,0:T(2,128)(2,1)S(1)} %get-tuple-element.23), channel_id=1, source_target_pairs={{0,1},{1,2},{2,3},{3,4},{4,5},{5,6},{6,7},{8,9},{9,10},{10,11},{11... | collective-permute-start | bytes 62216 | tf_op jit(solution)/shard_map/ppermute | solution.py:19
  162.8 6.5 collective-permute-start.3
  171.5 1.9 copy-start.5
  179.7 0.9 copy-start.6
  203.0 2.2 copy-start.2
  204.5 449.3 %all-gather.9.cloned.1.call-start = ((), (), s32[]{:S(2)}) async-start(), calls=%async_computation.2 | async-start | bytes 22118400 | tf_op jit(solution)/shard_map/all_gather | solution.py:96
  208.3 681.9 %all-gather.11.cloned.1.call-start = ((), (), s32[]{:S(2)}) async-start(), calls=%async_computation.3 | async-start | bytes 11796480 | tf_op jit(solution)/shard_map/all_gather | solution.py:107
  926.2 19.1 %copy-start.1 = (bf16[768,192]{0,1:T(8,128)(2,1)S(1)}, bf16[768,192]{0,1:T(8,128)(2,1)}, u32[]{:S(2)}) copy-start(bf16[768,192]{0,1:T(8,128)(2,1)} %param.13) | copy-start | bytes 884740
Sparse Core Ops, SparseCore 0:
  9.0 187.9 all-gather.4
  204.6 67.2 all-gather.6
  273.6 380.1 all-gather.8
  681.5 208.6 all-gather.10
